TPU v7x, 32 devices: a whole 2x2x4 slice. The times are simulated.
32 devices in a mesh: groups: 2 (over x), ctx: 16 (over z, y, core).
Axes of the slice: x: 2, y: 2, z: 4, core: 2. Of those that a mesh axis runs over, the one named last changes fastest.
Arguments:
- query_proj: bfloat16 [4096, 4096], P(('groups', 'ctx')), parts along dimension 0, may hold values from -6 to 6
- key_proj: bfloat16 [4096, 4096], P(('groups', 'ctx')), parts along dimension 0, may hold values from -6 to 6
- value_proj: bfloat16 [4096, 4096], P(('groups', 'ctx')), parts along dimension 0, may hold values from -6 to 6
- out_grad: bfloat16 [4096, 4096], P(('groups', 'ctx')), parts along dimension 0, may hold values from -6 to 6
- decay_rate: float32 [256, 16], replicated, may hold values from 0 to 0.034, as said below
- residue: float32 [256, 16], replicated, may hold values from -0.3 to 0.3
- group_of: int32 [4096], replicated, may hold values from 0 to 255, as said below
Outputs:
- hyena_out: bfloat16 [4096, 4096], P(('groups', 'ctx')), parts along dimension 0
- query_grad: bfloat16 [4096, 4096], P(('groups', 'ctx')), parts along dimension 0
- key_grad: bfloat16 [4096, 4096], P(('groups', 'ctx')), parts along dimension 0
- value_grad: bfloat16 [4096, 4096], P(('groups', 'ctx')), parts along dimension 0
- filter_update: float32 [512, 16], P('groups'), parts along dimension 0
There are 2 independent parts, one for each index of `groups`. A program takes and returns all parts, laid end to end along the dimension named above; an argument that names none is the same for every part. Nothing has to cross between parts.
Inputs may be any that keep to these rules, and one draw needn't show every extreme that they name: `group_of`: each of the 256 filter groups holds exactly 16 channels. `decay_rate`: positive rates.
All inputs are finite; a program needn't handle non-finite values.
Results may differ from a plain program's by a relative error of at most 0.005.
Values sent between devices are 32-bit elements; how exact they have to be, the bound alone decides.
No kernel may reach another device: no remote copies, remote signals or barrier semaphores. Data moves between devices by JAX's collectives and lax.ppermute only.
A program may use at most 192 MiB of HBM per device.

v0:
```python
import jax
import jax.numpy as jnp
from jax import lax
from jax.sharding import PartitionSpec as P


def carried_in(part, axis, combine, identity, reverse):
    count = lax.axis_size(axis)
    place = lax.axis_index(axis)
    ahead = count - 1 - place if reverse else place
    gathered = jax.tree.map(lambda a: lax.all_gather(a, axis), part)
    state = jax.tree.map(lambda a, e: jnp.zeros_like(a) + jnp.asarray(e, a.dtype), part, identity)

    def one(lap, state):
        source = count - 1 - lap if reverse else lap
        return combine(
            state, jax.tree.map(lambda a: lax.dynamic_index_in_dim(a, source, 0, False), gathered)
        )

    return lax.fori_loop(0, ahead, one, state)


def on_device(query_proj, key_proj, value_proj, out_grad, decay_rate, residue, group_of):
    high = lax.Precision.HIGHEST
    row_count, channel_count = query_proj.shape
    group_count, mode_count = decay_rate.shape
    per_group = channel_count // group_count
    order = jnp.argsort(group_of, stable=True)
    inverse = jnp.argsort(order, stable=True)
    query_f = query_proj.astype(jnp.float32)
    key_f = key_proj.astype(jnp.float32)
    value_f = value_proj.astype(jnp.float32)
    grad_f = out_grad.astype(jnp.float32)
    mixed = lax.optimization_barrier((key_f * value_f).astype(jnp.bfloat16))
    mixed_sorted = (
        jnp.take(mixed.T, order, axis=0)
        .astype(jnp.float32)
        .reshape(group_count, per_group, row_count)
    )
    upstream = grad_f * query_f
    upstream_sorted = jnp.take(upstream.T, order, axis=0).reshape(group_count, per_group, row_count)
    positions = jnp.arange(row_count, dtype=jnp.float32)
    powers = jnp.exp(-decay_rate[:, :, None] * positions[None, None, :])
    inverse_powers = jnp.exp(decay_rate[:, :, None] * positions[None, None, :])
    later_powers = powers * jnp.exp(-decay_rate)[:, :, None]
    reversed_powers = powers[:, :, ::-1]
    weighted = later_powers * residue[:, :, None]
    weighted_back = reversed_powers * residue[:, :, None]
    causal = (
        jnp.arange(row_count, dtype=jnp.int32)[:, None]
        >= jnp.arange(row_count, dtype=jnp.int32)[None, :]
    )
    toeplitz = jnp.einsum(
        "gmt,gms->gts", powers * residue[:, :, None], inverse_powers, precision=high
    )
    toeplitz = jnp.where(causal[None], toeplitz, 0.0)
    local_out = jnp.einsum("gts,gcs->gct", toeplitz, mixed_sorted, precision=high)
    local_back = jnp.einsum("gts,gct->gcs", toeplitz, upstream_sorted, precision=high)
    end_state = jnp.einsum("gms,gcs->mgc", reversed_powers, mixed_sorted, precision=high).reshape(
        mode_count, channel_count
    )
    head_term = jnp.einsum("gmt,gct->mgc", later_powers, upstream_sorted, precision=high).reshape(
        mode_count, channel_count
    )
    empty_state = jnp.zeros((mode_count, channel_count), jnp.float32)
    group_decay = jnp.exp(-decay_rate * row_count).T
    unit_decay = jnp.ones_like(group_decay)

    def chain_decays(earlier, later):
        widened = jnp.repeat(later[0], per_group, axis=1)
        return (earlier[0] * later[0], widened * earlier[1] + later[1])

    carry_pair = carried_in(
        (group_decay, end_state), "ctx", chain_decays, (unit_decay, empty_state), False
    )
    back_pair = carried_in(
        (group_decay, head_term), "ctx", chain_decays, (unit_decay, empty_state), True
    )
    carry_in = carry_pair[1]
    carry_back = back_pair[1]
    carry_grouped = carry_in.reshape(mode_count, group_count, per_group)
    back_grouped = carry_back.reshape(mode_count, group_count, per_group)
    out_sorted = local_out + jnp.einsum("gmt,mgc->gct", weighted, carry_grouped, precision=high)
    back_sorted = local_back + jnp.einsum(
        "gms,mgc->gcs", weighted_back, back_grouped, precision=high
    )
    cross = jnp.einsum("gct,gcs->gts", upstream_sorted, mixed_sorted, precision=high)
    cross = jnp.where(causal[None], cross, 0.0)
    inner = jnp.einsum("gts,gms->gmt", cross, inverse_powers, precision=high)
    local_grad = jnp.sum(inner * powers, axis=2)
    local_grad = (
        local_grad
        + jnp.sum((carry_in * head_term).reshape(mode_count, group_count, per_group), axis=2).T
    )
    filter_grad = lax.psum(local_grad, "ctx")
    filter_update = filter_grad / jnp.sqrt(jnp.mean(filter_grad * filter_grad) + 1e-06)
    filtered = jnp.take(out_sorted.reshape(channel_count, row_count), inverse, axis=0).T
    mixed_grad = jnp.take(back_sorted.reshape(channel_count, row_count), inverse, axis=0).T
    hyena_out = (query_f * filtered).astype(jnp.bfloat16)
    query_grad = (grad_f * filtered).astype(jnp.bfloat16)
    key_grad = (mixed_grad * value_f).astype(jnp.bfloat16)
    value_grad = (mixed_grad * key_f).astype(jnp.bfloat16)
    return (hyena_out, query_grad, key_grad, value_grad, filter_update)


def solution(mesh):
    placed = (
        P(("groups", "ctx"), None),
        P(("groups", "ctx"), None),
        P(("groups", "ctx"), None),
        P(("groups", "ctx"), None),
        P(),
        P(),
        P(),
    )
    return jax.shard_map(
        on_device,
        mesh=mesh,
        in_specs=placed,
        out_specs=(
            P(("groups", "ctx"), None),
            P(("groups", "ctx"), None),
            P(("groups", "ctx"), None),
            P(("groups", "ctx"), None),
            P("groups", None),
        ),
        check_vma=False,
    )
```

profile of v0, /device:TPU:0, one launch (start us, length us, event | category | flops | bytes accessed | tf_op | source)
XLA Modules:
  0.0 484.3 jit_solution(5520543099957598316)
XLA Ops:
  7.2 6.6 %sort.31 = (s32[4096]{0:T(1024)}, s32[4096]{0:T(1024)S(1)}) sort(s32[4096]{0:T(1024)} %param.19, s32[4096]{0:T(1024)S(1)} %iota.26), dimensions={0}, to_apply=%region_0.0 | sort | flops 49152 | bytes 65536 | tf_op jit(solution)/shard_map/jit(argsort)/sort | solution.py:28
  22.7 15.0 %gather_fusion = bf16[4096,128]{1,0:T(8,128)(2,1)} fusion(bf16[4096,128]{1,0:T(8,128)(2,1)S(1)} %bitcast.52, s32[4096]{0:T(1024)S(1)} %fusion.51), kind=kCustom, calls=%fused_computation.3 | custom fusion | bytes 2113536 | tf_op jit(solution)/shard_map/jit(_take)/gather | solution.py:36
  37.7 4.5 fusion.47
  42.2 3.0 copy.70
  45.4 5.8 %sort.32 = (s32[4096]{0:T(1024)}, s32[4096]{0:T(1024)S(1)}) sort(s32[4096]{0:T(1024)S(1)} %get-tuple-element.136, s32[4096]{0:T(1024)S(1)} %iota.27), dimensions={0}, to_apply=%region_3.4 | sort | flops 49152 | bytes 65536 | tf_op jit(solution)/shard_map/jit(argsort)/sort | solution.py:29
  54.7 26.0 %all-gather = f32[256,256]{1,0:T(8,128)} all-gather(f32[16,256]{1,0:T(8,128)S(1)} %get-tuple-element.186), channel_id=2, replica_groups=mesh['groups'=2,'ctx'=16] {'ctx'}, dimensions={0}, use_global_device_ids=true | all-gather | bytes 278528 | tf_op jit(solution)/shard_map/all_gather | solution.py:11
  81.9 28.7 %fusion.22 = f32[256,128,128]{2,1,0:T(8,128)S(1)} fusion(f32[256,16]{1,0:T(8,128)S(1)} %copy.69, f32[256,16]{1,0:T(8,128)S(1)} %copy.68, f32[256,16]{1,0:T(8,128)S(1)} %copy.67), kind=kOutput, calls=%fused_computation.38 | convolution fusion | flops 806879232 | bytes 16826368 | tf_op jit(solution)/shard_map/gmt,gms->gts/dot_general | solution.py:53
  110.6 5.7 %copy-done = f32[256,128,128]{2,1,0:T(8,128)} copy-done((f32[256,128,128]{2,1,0:T(8,128)}, f32[256,128,128]{2,1,0:T(8,128)S(1)}, u32[]{:S(2)}) %copy-start) | copy-done | bytes 16777240
  116.3 14.5 %fusion.4 = f32[256,16,128]{2,1,0:T(8,128)} fusion(f32[256,128,128]{2,1,0:T(8,128)S(1)} %fusion.22, pred[128,128]{1,0:T(8,128)(4,1)S(1)} %iota_compare_fusion, bf16[256,16,128]{2,1,0:T(8,128)(2,1)S(1)} %bitcast.59, pred[256,16]{1,0:T(8,128)(4,1)S(1)} %copy-done.17), kind=kOutput, calls=%fused_computation.12 | convolution fusion | flops 810024960 | bytes 19943424 | tf_op jit(solution)/shard_map/gts,gcs->gct/dot_general | solution.py:57
  134.6 5.0 %fusion.28 = f32[256,16,128]{2,1,0:T(8,128)S(1)} fusion(f32[256,16,128]{2,1,0:T(8,128)} %fusion.4, f32[16,256,16]{0,2,1:T(8,128)} %bitcast.61, f32[256,16]{1,0:T(8,128)S(1)} %copy-done.12, f32[256,16]{1,0:T(8,128)S(1)} %copy-done.10, f32[256,16]{1,0:T(8,128)S(1)} %copy.67), kind=kOutput, calls=%fused_computation.43 | convolution fusion | flops 102760448 | bytes 4505600 | tf_op jit(solution)/shard_map/gmt,mgc->gct/dot_general | solution.py:83
  139.6 15.5 %gather_fusion.1 = f32[4096,128]{1,0:T(8,128)} fusion(f32[4096,128]{1,0:T(8,128)S(1)} %bitcast.50, s32[4096]{0:T(1024)} %fusion.52), kind=kCustom, calls=%fused_computation.clone | custom fusion | bytes 4210688 | tf_op jit(solution)/shard_map/jit(_take)/gather | solution.py:97
  155.1 5.1 %fusion.16 = (bf16[128,4096]{0,1:T(8,128)(2,1)}, bf16[128,4096]{0,1:T(8,128)(2,1)}, f32[4096,128]{1,0:T(8,128)S(1)}) fusion(bf16[128,4096]{0,1:T(8,128)(2,1)} %copy.73, f32[4096,128]{1,0:T(8,128)} %gather_fusion.1, pred[4096]{0:T(1024)(128)(4,1)S(1)} %copy-done.26, bf16[128,4096]{0,1:T(8,128)(2,1)} %copy.64), kind=kLoop, calls=%fused_computation.30 | loop fusion | flops 4194304 | bytes 8392704 | tf_op jit(solution)/shard_map/convert_element_type | solution.py:100
  160.2 14.2 %gather_fusion.2 = f32[4096,128]{1,0:T(8,128)} fusion(f32[4096,128]{1,0:T(8,128)S(1)} %get-tuple-element.184, s32[4096]{0:T(1024)S(1)} %copy-done.21), kind=kCustom, calls=%fused_computation.1.clone | custom fusion | bytes 4210688 | tf_op jit(solution)/shard_map/jit(_take)/gather | solution.py:41
  174.4 3.6 broadcast_select_fusion
  178.0 5.4 %fusion.25 = f32[256,16,16]{2,1,0:T(8,128)} fusion(f32[256,16,128]{2,1,0:T(8,128)S(1)} %bitcast.53, f32[256,16]{1,0:T(8,128)S(1)} %copy-done.12, f32[256,16]{1,0:T(8,128)S(1)} %copy.67), kind=kOutput, calls=%fused_computation.42 | convolution fusion | flops 101711872 | bytes 2392064 | tf_op jit(solution)/shard_map/gmt,gct->mgc/dot_general | solution.py:62
  195.8 3.0 reshape.82
  201.8 13.9 %fusion.46 = f32[256,128,128]{2,1,0:T(8,128)S(1)} fusion(f32[256,16,128]{2,1,0:T(8,128)S(1)} %bitcast.54, bf16[256,16,128]{2,1,0:T(8,128)(2,1)S(1)} %bitcast.60, pred[256,16]{1,0:T(8,128)(4,1)S(1)} %copy-done.18), kind=kOutput, calls=%fused_computation.57 | convolution fusion | flops 805830656 | bytes 19927040 | tf_op jit(solution)/shard_map/gct,gcs->gts/dot_general | solution.py:87
  215.7 26.9 %multiply_reduce_fusion = f32[256,16]{1,0:T(8,128)S(1)} fusion(f32[256,16]{1,0:T(8,128)S(1)} %copy.67, f32[256,128,128]{2,1,0:T(8,128)S(1)} %fusion.46, pred[128,128]{1,0:T(8,128)(4,1)S(1)} %iota_compare_fusion, f32[256,16]{1,0:T(8,128)S(1)} %copy-done.8), kind=kOutput, calls=%fused_computation.32 | convolution fusion | flops 811593728 | bytes 16842752 | tf_op jit(solution)/shard_map/gts,gms->gmt/dot_general | solution.py:89
  242.6 127.4 %psum.7 = f32[256,16]{1,0:T(8,128)S(1)} all-reduce(f32[256,16]{1,0:T(8,128)S(1)} %bitcast_add_fusion.2), channel_id=1, replica_groups=mesh['groups'=2,'ctx'=16] {'ctx'}, use_global_device_ids=true, to_apply=%region_8.10 | all-reduce | flops 4096 | bytes 32768 | tf_op jit(solution)/shard_map/psum | solution.py:95
  372.1 17.6 %fusion.2 = f32[256,16,128]{2,1,0:T(8,128)} fusion(f32[256,16,128]{2,1,0:T(8,128)S(1)} %bitcast.55, f32[256,128,128]{2,1,0:T(8,128)} %copy-done, pred[128,128]{1,0:T(8,128)(4,1)S(1)} %iota_compare_fusion), kind=kOutput, calls=%fused_computation.10 | convolution fusion | flops 809500672 | bytes 20987904 | tf_op jit(solution)/shard_map/gts,gct->gcs/dot_general | solution.py:58
  389.7 59.8 %while.27 = (s32[]{:T(128)}, f32[16,4096]{1,0:T(8,128)S(1)}, s32[]{:T(128)}, f32[16,16,256]{2,1,0:T(8,128)}, f32[16,16,4096]{2,1,0:T(8,128)}, /*index=5*/s32[]{:T(128)}, s32[]{:T(128)}, s32[]{:T(128)}, s32[]{:T(128)}) while((s32[]{:T(128)}, f32[16,4096]{1,0:T(8,128)S(1)}, s32[]{:T(128)}, f32[16,16,256]{2,1,0:T(8,128)}, ...), condition=%wide.region_5.7_spmd, body=%wide.region_4.6_spmd.sunk | while | flops 131078 | bytes 1884315 | solution.py:20
  451.4 5.1 %fusion.31 = f32[256,16,128]{2,1,0:T(8,128)S(1)} fusion(f32[256,16,128]{2,1,0:T(8,128)} %fusion.2, f32[16,256,16]{0,2,1:T(8,128)} %bitcast.63, f32[256,16,128]{2,1,0:T(8,128)} %copy-done.1, f32[256,16]{1,0:T(8,128)S(1)} %copy-done.11), kind=kOutput, calls=%fused_computation.44 | convolution fusion | flops 101711872 | bytes 6569984 | tf_op jit(solution)/shard_map/gms,mgc->gcs/dot_general | solution.py:84
  456.6 14.2 %gather_fusion.3 = f32[4096,128]{1,0:T(8,128)} fusion(f32[4096,128]{1,0:T(8,128)S(1)} %bitcast.51, s32[4096]{0:T(1024)S(1)} %copy-done.22), kind=kCustom, calls=%fused_computation.2.clone | custom fusion | bytes 4210688 | tf_op jit(solution)/shard_map/jit(_take)/gather | solution.py:98
  470.8 3.8 fusion.13
  (161 shorter events, 98.3 us)
Async XLA Ops:
  7.2 9.3 %copy-start.13 = (bf16[128,4096]{1,0:T(8,128)(2,1)S(1)}, bf16[128,4096]{1,0:T(8,128)(2,1)}, u32[]{:S(2)}) copy-start(bf16[128,4096]{1,0:T(8,128)(2,1)} %param.15) | copy-start | bytes 3145732
  7.2 123.6 %all-gather.4.cloned.1.call-start = ((), (), s32[]{:S(2)}) async-start(), calls=%async_computation | async-start | bytes 4456448 | tf_op jit(solution)/shard_map/all_gather | solution.py:11
  13.8 8.8 %copy-start.20 = (s32[4096]{0:T(1024)}, s32[4096]{0:T(1024)S(1)}, u32[]{:S(2)}) copy-start(s32[4096]{0:T(1024)S(1)} %fusion.51) | copy-start | bytes 49156
  14.0 23.7 %copy-start.16 = (pred[256,16]{1,0:T(8,128)(4,1)}, pred[256,16]{1,0:T(8,128)(4,1)S(1)}, u32[]{:S(2)}) copy-start(pred[256,16]{1,0:T(8,128)(4,1)S(1)} %broadcast_in_dim.68) | copy-start | bytes 12292
  22.6 15.1 %copy-start.1 = (f32[256,16,128]{2,1,0:T(8,128)}, f32[256,16,128]{2,1,0:T(8,128)S(1)}, u32[]{:S(2)}) copy-start(f32[256,16,128]{2,1,0:T(8,128)S(1)} %rev.3) | copy-start | bytes 6291460
  42.2 9.8 %copy-start.28 = (f32[256,16]{0,1:T(8,128)S(1)}, f32[256,16]{0,1:T(8,128)}, u32[]{:S(2)}) copy-start(f32[256,16]{0,1:T(8,128)} %param.18) | copy-start | bytes 49156
  42.2 9.9 %copy-start.14 = (bf16[128,4096]{1,0:T(8,128)(2,1)S(1)}, bf16[128,4096]{1,0:T(8,128)(2,1)}, u32[]{:S(2)}) copy-start(bf16[128,4096]{1,0:T(8,128)(2,1)} %param.13) | copy-start | bytes 3145732
  42.2 11.2 %copy-start.15 = (bf16[128,4096]{1,0:T(8,128)(2,1)S(1)}, bf16[128,4096]{1,0:T(8,128)(2,1)}, u32[]{:S(2)}) copy-start(bf16[128,4096]{1,0:T(8,128)(2,1)} %param.16) | copy-start | bytes 3145732
  45.2 344.4 %all-gather.6.cloned.1.call-start = ((), (), s32[]{:S(2)}) async-start(), calls=%async_computation.1 | async-start | bytes 4456448 | tf_op jit(solution)/shard_map/all_gather | solution.py:11
  45.4 36.5 %copy-start.7 = (f32[256,16]{1,0:T(8,128)}, f32[256,16]{1,0:T(8,128)S(1)}, u32[]{:S(2)}) copy-start(f32[256,16]{1,0:T(8,128)S(1)} %copy.69) | copy-start | bytes 49156
  52.0 29.8 %copy-start.9 = (f32[256,16]{1,0:T(8,128)}, f32[256,16]{1,0:T(8,128)S(1)}, u32[]{:S(2)}) copy-start(f32[256,16]{1,0:T(8,128)S(1)} %copy.68) | copy-start | bytes 49156
  81.9 34.4 %copy-start.2 = (bf16[4096,128]{1,0:T(8,128)(2,1)S(1)}, bf16[4096,128]{1,0:T(8,128)(2,1)}, u32[]{:S(2)}) copy-start(bf16[4096,128]{1,0:T(8,128)(2,1)} %gather_fusion) | copy-start | bytes 3145732
  81.9 34.4 %copy-start.17 = (pred[256,16]{1,0:T(8,128)(4,1)S(1)}, pred[256,16]{1,0:T(8,128)(4,1)}, u32[]{:S(2)}) copy-start(pred[256,16]{1,0:T(8,128)(4,1)} %copy-done.16) | copy-start | bytes 12292
  110.6 5.7 %copy-start = (f32[256,128,128]{2,1,0:T(8,128)}, f32[256,128,128]{2,1,0:T(8,128)S(1)}, u32[]{:S(2)}) copy-start(f32[256,128,128]{2,1,0:T(8,128)S(1)} %fusion.22) | copy-start | bytes 50331652
  139.6 15.5 %copy-start.26 = (pred[4096]{0:T(1024)(128)(4,1)S(1)}, pred[4096]{0:T(1024)(128)(4,1)}, u32[]{:S(2)}) copy-start(pred[4096]{0:T(1024)(128)(4,1)} %compare_and_fusion) | copy-start | bytes 12292
  155.1 5.1 %copy-start.21 = (s32[4096]{0:T(1024)S(1)}, s32[4096]{0:T(1024)}, u32[]{:S(2)}) copy-start(s32[4096]{0:T(1024)} %copy-done.20) | copy-start | bytes 49156
  160.2 14.2 %copy-start.25 = (pred[4096]{0:T(1024)(128)(4,1)S(1)}, pred[4096]{0:T(1024)(128)(4,1)}, u32[]{:S(2)}) copy-start(pred[4096]{0:T(1024)(128)(4,1)} %copy-done.24) | copy-start | bytes 12292
  188.5 5.6 %copy-start.3 = (f32[16,4096]{1,0:T(8,128)S(1)}, f32[16,4096]{1,0:T(8,128)}, u32[]{:S(2)}) copy-start(f32[16,4096]{1,0:T(8,128)} %get-tuple-element.137) | copy-start | bytes 786436
  195.8 6.0 %copy-start.18 = (pred[256,16]{1,0:T(8,128)(4,1)S(1)}, pred[256,16]{1,0:T(8,128)(4,1)}, u32[]{:S(2)}) copy-start(pred[256,16]{1,0:T(8,128)(4,1)} %copy-done.16) | copy-start | bytes 12292
  201.8 13.9 %copy-start.8 = (f32[256,16]{1,0:T(8,128)S(1)}, f32[256,16]{1,0:T(8,128)}, u32[]{:S(2)}) copy-start(f32[256,16]{1,0:T(8,128)} %copy-done.7) | copy-start | bytes 49156
  215.7 26.9 %copy-start.19 = (f32[16,256]{0,1:T(8,128)S(1)}, f32[16,256]{0,1:T(8,128)}, u32[]{:S(2)}) copy-start(f32[16,256]{0,1:T(8,128)} %copy.77) | copy-start | bytes 49156
  451.4 5.1 %copy-start.22 = (s32[4096]{0:T(1024)S(1)}, s32[4096]{0:T(1024)}, u32[]{:S(2)}) copy-start(s32[4096]{0:T(1024)} %fusion.52) | copy-start | bytes 49156
  456.6 14.2 %copy-start.5 = (bf16[128,4096]{0,1:T(8,128)(2,1)S(1)}, bf16[128,4096]{0,1:T(8,128)(2,1)}, u32[]{:S(2)}) copy-start(bf16[128,4096]{0,1:T(8,128)(2,1)} %copy-done.4) | copy-start | bytes 3145732
  456.6 14.2 %copy-start.27 = (pred[4096]{0:T(1024)(128)(4,1)S(1)}, pred[4096]{0:T(1024)(128)(4,1)}, u32[]{:S(2)}) copy-start(pred[4096]{0:T(1024)(128)(4,1)} %compare_and_fusion) | copy-start | bytes 12292
  (7 other events, 13.9 us)
Sparse Core Ops, SparseCore 0:
  45.3 53.8 all-gather.3
  186.4 116.4 all-gather.5
where the time goes:
time: 493 us; the launch traced here: 484 us
  blocking collectives  153 us (31%)
  local copies, waits for them, and re-layouts  144 us (29%)
  matrix products  121 us (25%)
  other arithmetic  49.6 us (10%)
  between operations  15.4 us (3%)
    psum x1, blocking collectives, on_device(): filter_grad = lax.psum(local_grad, 'ctx')  127 us
    dot_general x1, matrix products, on_device(): jnp.einsum('gmt,gms->gts', powers * residue[:, :, None], inverse_powers,...  28.7 us
    dot_general x1, matrix products, on_device(): inner = jnp.einsum('gts,gms->gmt', cross, inverse_powers, precision=high)  26.9 us
    all_gather x1, blocking collectives, carried_in(): gathered = jax.tree.map(lambda a: lax.all_gather(a, axis), part)  26 us
    reshape x15, local copies, waits for them, and re-layouts, chain_decays(): widened = jnp.repeat(later[0], per_group, axis=1)  23.4 us
    unnamed x69, local copies, waits for them, and re-layouts  19.9 us
    dot_general x1, matrix products, on_device(): jnp.einsum('gts,gct->gcs', toeplitz, upstream_sorted, precision=high)  17.6 us
    add x15, other arithmetic, chain_decays(): return (earlier[0] * later[0], widened * earlier[1] + later[1])  16.3 us
  transfers between devices with their start and end apart: 2, of which 0 were waited for; matrix products, arithmetic and copies ran while one was open for 27% of the time, Pallas kernels for 0%

commit v1 on v0

--- a/solution.py
+++ b/solution.py
@@ -92,7 +92,7 @@
         local_grad
         + jnp.sum((carry_in * head_term).reshape(mode_count, group_count, per_group), axis=2).T
     )
-    filter_grad = lax.psum(local_grad, "ctx")
+    filter_grad = jnp.sum(lax.all_gather(local_grad, "ctx"), axis=0)
     filter_update = filter_grad / jnp.sqrt(jnp.mean(filter_grad * filter_grad) + 1e-06)
     filtered = jnp.take(out_sorted.reshape(channel_count, row_count), inverse, axis=0).T
     mixed_grad = jnp.take(back_sorted.reshape(channel_count, row_count), inverse, axis=0).T

time: 493 us -> 462 us (0.937)
  blocking collectives: 153 us -> 121 us
    psum x1 -> x0, blocking collectives: 127 us -> none  [on_device(): filter_grad = lax.psum(local_grad, 'ctx')]
    all_gather x0 -> x1, blocking collectives: none -> 94.7 us  [on_device(): filter_grad = jnp.sum(lax.all_gather(local_grad, 'ctx'), axis=0)]
  transfers between devices with their start and end apart: 2 -> 2, of which waited for: 0 -> 0; matrix products, arithmetic and copies ran while one was open for 27% -> 29% of each run, Pallas kernels for 0% -> 0%
where the time goes in v1:
time: 462 us; the launch traced here: 454 us
  local copies, waits for them, and re-layouts  144 us (31%)
  matrix products  122 us (26%)
  blocking collectives  121 us (26%)
  other arithmetic  51.4 us (11%)
  between operations  15.4 us (3%)
    all_gather x1, blocking collectives, on_device(): filter_grad = jnp.sum(lax.all_gather(local_grad, 'ctx'), axis=0)  94.7 us
    dot_general x1, matrix products, on_device(): jnp.einsum('gmt,gms->gts', powers * residue[:, :, None], inverse_powers,...  28.7 us
    dot_general x1, matrix products, on_device(): inner = jnp.einsum('gts,gms->gmt', cross, inverse_powers, precision=high)  26.9 us
    all_gather x1, blocking collectives, carried_in(): gathered = jax.tree.map(lambda a: lax.all_gather(a, axis), part)  26 us
    reshape x15, local copies, waits for them, and re-layouts, chain_decays(): widened = jnp.repeat(later[0], per_group, axis=1)  23.4 us
    unnamed x69, local copies, waits for them, and re-layouts  19.9 us
    dot_general x1, matrix products, on_device(): jnp.einsum('gts,gct->gcs', toeplitz, upstream_sorted, precision=high)  17.8 us
    add x15, other arithmetic, chain_decays(): return (earlier[0] * later[0], widened * earlier[1] + later[1])  16.3 us
  transfers between devices with their start and end apart: 2, of which 0 were waited for; matrix products, arithmetic and copies ran while one was open for 29% of the time, Pallas kernels for 0%

profile of v1, /device:TPU:0, one launch (start us, length us, event | category | flops | bytes accessed | tf_op | source)
XLA Modules:
  0.0 453.6 jit_solution(8318456461130630483)
XLA Ops:
  7.2 6.6 %sort.31 = (s32[4096]{0:T(1024)}, s32[4096]{0:T(1024)S(1)}) sort(s32[4096]{0:T(1024)} %param.19, s32[4096]{0:T(1024)S(1)} %iota.26), dimensions={0}, to_apply=%region_0.0 | sort | flops 49152 | bytes 65536 | tf_op jit(solution)/shard_map/jit(argsort)/sort | solution.py:28
  22.7 15.0 %gather_fusion = bf16[4096,128]{1,0:T(8,128)(2,1)} fusion(bf16[4096,128]{1,0:T(8,128)(2,1)S(1)} %bitcast.53, s32[4096]{0:T(1024)S(1)} %fusion.51), kind=kCustom, calls=%fused_computation.3 | custom fusion | bytes 2113536 | tf_op jit(solution)/shard_map/jit(_take)/gather | solution.py:36
  37.7 4.5 fusion.47
  42.2 3.0 copy.87
  45.4 5.8 %sort.32 = (s32[4096]{0:T(1024)}, s32[4096]{0:T(1024)S(1)}) sort(s32[4096]{0:T(1024)S(1)} %get-tuple-element.136, s32[4096]{0:T(1024)S(1)} %iota.27), dimensions={0}, to_apply=%region_3.4 | sort | flops 49152 | bytes 65536 | tf_op jit(solution)/shard_map/jit(argsort)/sort | solution.py:29
  54.7 26.0 %all-gather = f32[256,256]{1,0:T(8,128)} all-gather(f32[16,256]{1,0:T(8,128)S(1)} %get-tuple-element.191), channel_id=2, replica_groups=mesh['groups'=2,'ctx'=16] {'ctx'}, dimensions={0}, use_global_device_ids=true | all-gather | bytes 278528 | tf_op jit(solution)/shard_map/all_gather | solution.py:11
  81.9 28.7 %fusion.22 = f32[256,128,128]{2,1,0:T(8,128)S(1)} fusion(f32[256,16]{1,0:T(8,128)S(1)} %copy.86, f32[256,16]{1,0:T(8,128)S(1)} %copy.85, f32[256,16]{1,0:T(8,128)S(1)} %copy.84), kind=kOutput, calls=%fused_computation.38 | convolution fusion | flops 806879232 | bytes 16826368 | tf_op jit(solution)/shard_map/gmt,gms->gts/dot_general | solution.py:53
  110.6 5.7 %copy-done = f32[256,128,128]{2,1,0:T(8,128)} copy-done((f32[256,128,128]{2,1,0:T(8,128)}, f32[256,128,128]{2,1,0:T(8,128)S(1)}, u32[]{:S(2)}) %copy-start) | copy-done | bytes 16777240
  116.3 14.5 %fusion.4 = f32[256,16,128]{2,1,0:T(8,128)} fusion(f32[256,128,128]{2,1,0:T(8,128)S(1)} %fusion.22, pred[128,128]{1,0:T(8,128)(4,1)S(1)} %iota_compare_fusion, bf16[256,16,128]{2,1,0:T(8,128)(2,1)S(1)} %bitcast.60, pred[256,16]{1,0:T(8,128)(4,1)S(1)} %copy-done.17), kind=kOutput, calls=%fused_computation.12 | convolution fusion | flops 810024960 | bytes 19943424 | tf_op jit(solution)/shard_map/gts,gcs->gct/dot_general | solution.py:57
  134.6 5.0 %fusion.28 = f32[256,16,128]{2,1,0:T(8,128)S(1)} fusion(f32[256,16,128]{2,1,0:T(8,128)} %fusion.4, f32[16,256,16]{0,2,1:T(8,128)} %bitcast.62, f32[256,16]{1,0:T(8,128)S(1)} %copy-done.12, f32[256,16]{1,0:T(8,128)S(1)} %copy-done.10, f32[256,16]{1,0:T(8,128)S(1)} %copy.84), kind=kOutput, calls=%fused_computation.43 | convolution fusion | flops 102760448 | bytes 4505600 | tf_op jit(solution)/shard_map/gmt,mgc->gct/dot_general | solution.py:83
  139.6 15.5 %gather_fusion.1 = f32[4096,128]{1,0:T(8,128)} fusion(f32[4096,128]{1,0:T(8,128)S(1)} %bitcast.51, s32[4096]{0:T(1024)} %fusion.52), kind=kCustom, calls=%fused_computation.clone | custom fusion | bytes 4210688 | tf_op jit(solution)/shard_map/jit(_take)/gather | solution.py:97
  155.1 5.1 %fusion.16 = (bf16[128,4096]{0,1:T(8,128)(2,1)}, bf16[128,4096]{0,1:T(8,128)(2,1)}, f32[4096,128]{1,0:T(8,128)S(1)}) fusion(bf16[128,4096]{0,1:T(8,128)(2,1)} %copy.90, f32[4096,128]{1,0:T(8,128)} %gather_fusion.1, pred[4096]{0:T(1024)(128)(4,1)S(1)} %copy-done.26, bf16[128,4096]{0,1:T(8,128)(2,1)} %copy.81), kind=kLoop, calls=%fused_computation.30 | loop fusion | flops 4194304 | bytes 8392704 | tf_op jit(solution)/shard_map/convert_element_type | solution.py:100
  160.2 14.2 %gather_fusion.2 = f32[4096,128]{1,0:T(8,128)} fusion(f32[4096,128]{1,0:T(8,128)S(1)} %get-tuple-element.189, s32[4096]{0:T(1024)S(1)} %copy-done.21), kind=kCustom, calls=%fused_computation.1.clone | custom fusion | bytes 4210688 | tf_op jit(solution)/shard_map/jit(_take)/gather | solution.py:41
  174.4 3.6 broadcast_select_fusion
  178.0 5.4 %fusion.25 = f32[256,16,16]{2,1,0:T(8,128)} fusion(f32[256,16,128]{2,1,0:T(8,128)S(1)} %bitcast.54, f32[256,16]{1,0:T(8,128)S(1)} %copy-done.12, f32[256,16]{1,0:T(8,128)S(1)} %copy.84), kind=kOutput, calls=%fused_computation.42 | convolution fusion | flops 101711872 | bytes 2392064 | tf_op jit(solution)/shard_map/gmt,gct->mgc/dot_general | solution.py:62
  195.8 3.0 reshape.82
  201.8 13.9 %fusion.46 = f32[256,128,128]{2,1,0:T(8,128)S(1)} fusion(f32[256,16,128]{2,1,0:T(8,128)S(1)} %bitcast.55, bf16[256,16,128]{2,1,0:T(8,128)(2,1)S(1)} %bitcast.61, pred[256,16]{1,0:T(8,128)(4,1)S(1)} %copy-done.18), kind=kOutput, calls=%fused_computation.57 | convolution fusion | flops 805830656 | bytes 19927040 | tf_op jit(solution)/shard_map/gct,gcs->gts/dot_general | solution.py:87
  215.7 26.9 %multiply_reduce_fusion = f32[256,16]{1,0:T(8,128)S(1)} fusion(f32[256,16]{1,0:T(8,128)S(1)} %copy.84, f32[256,128,128]{2,1,0:T(8,128)S(1)} %fusion.46, pred[128,128]{1,0:T(8,128)(4,1)S(1)} %iota_compare_fusion, f32[256,16]{1,0:T(8,128)S(1)} %copy-done.8), kind=kOutput, calls=%fused_computation.32 | convolution fusion | flops 811593728 | bytes 16842752 | tf_op jit(solution)/shard_map/gts,gms->gmt/dot_general | solution.py:89
  242.6 94.7 %all-gather.1 = f32[4096,16]{1,0:T(8,128)} all-gather(f32[256,16]{1,0:T(8,128)S(1)} %bitcast_add_fusion.2), channel_id=3, replica_groups=mesh['groups'=2,'ctx'=16] {'ctx'}, dimensions={0}, use_global_device_ids=true | all-gather | bytes 278528 | tf_op jit(solution)/shard_map/all_gather | solution.py:95
  341.2 17.8 %fusion.2 = f32[256,16,128]{2,1,0:T(8,128)} fusion(f32[256,16,128]{2,1,0:T(8,128)S(1)} %bitcast.56, f32[256,128,128]{2,1,0:T(8,128)} %copy-done, pred[128,128]{1,0:T(8,128)(4,1)S(1)} %iota_compare_fusion), kind=kOutput, calls=%fused_computation.10 | convolution fusion | flops 809500672 | bytes 20987904 | tf_op jit(solution)/shard_map/gts,gct->gcs/dot_general | solution.py:58
  359.0 59.8 %while.27 = (s32[]{:T(128)}, f32[16,4096]{1,0:T(8,128)S(1)}, s32[]{:T(128)}, f32[16,16,256]{2,1,0:T(8,128)}, f32[16,16,4096]{2,1,0:T(8,128)}, /*index=5*/s32[]{:T(128)}, s32[]{:T(128)}, s32[]{:T(128)}, s32[]{:T(128)}) while((s32[]{:T(128)}, f32[16,4096]{1,0:T(8,128)S(1)}, s32[]{:T(128)}, f32[16,16,256]{2,1,0:T(8,128)}, ...), condition=%wide.region_5.7_spmd, body=%wide.region_4.6_spmd.sunk | while | flops 131078 | bytes 1884315 | solution.py:20
  420.7 5.1 %fusion.31 = f32[256,16,128]{2,1,0:T(8,128)S(1)} fusion(f32[256,16,128]{2,1,0:T(8,128)} %fusion.2, f32[16,256,16]{0,2,1:T(8,128)} %bitcast.65, f32[256,16,128]{2,1,0:T(8,128)} %copy-done.1, f32[256,16]{1,0:T(8,128)S(1)} %copy-done.11), kind=kOutput, calls=%fused_computation.44 | convolution fusion | flops 101711872 | bytes 6569984 | tf_op jit(solution)/shard_map/gms,mgc->gcs/dot_general | solution.py:84
  425.9 14.2 %gather_fusion.3 = f32[4096,128]{1,0:T(8,128)} fusion(f32[4096,128]{1,0:T(8,128)S(1)} %bitcast.52, s32[4096]{0:T(1024)S(1)} %copy-done.22), kind=kCustom, calls=%fused_computation.2.clone | custom fusion | bytes 4210688 | tf_op jit(solution)/shard_map/jit(_take)/gather | solution.py:98
  440.1 3.8 fusion.13
  (162 shorter events, 100.0 us)
Async XLA Ops:
  7.2 9.3 %copy-start.13 = (bf16[128,4096]{1,0:T(8,128)(2,1)S(1)}, bf16[128,4096]{1,0:T(8,128)(2,1)}, u32[]{:S(2)}) copy-start(bf16[128,4096]{1,0:T(8,128)(2,1)} %param.15) | copy-start | bytes 3145732
  7.2 123.6 %all-gather.5.cloned.1.call-start = ((), (), s32[]{:S(2)}) async-start(), calls=%async_computation | async-start | bytes 4456448 | tf_op jit(solution)/shard_map/all_gather | solution.py:11
  13.8 8.8 %copy-start.20 = (s32[4096]{0:T(1024)}, s32[4096]{0:T(1024)S(1)}, u32[]{:S(2)}) copy-start(s32[4096]{0:T(1024)S(1)} %fusion.51) | copy-start | bytes 49156
  14.0 23.7 %copy-start.16 = (pred[256,16]{1,0:T(8,128)(4,1)}, pred[256,16]{1,0:T(8,128)(4,1)S(1)}, u32[]{:S(2)}) copy-start(pred[256,16]{1,0:T(8,128)(4,1)S(1)} %broadcast_in_dim.68) | copy-start | bytes 12292
  22.6 15.1 %copy-start.1 = (f32[256,16,128]{2,1,0:T(8,128)}, f32[256,16,128]{2,1,0:T(8,128)S(1)}, u32[]{:S(2)}) copy-start(f32[256,16,128]{2,1,0:T(8,128)S(1)} %rev.3) | copy-start | bytes 6291460
  42.2 9.8 %copy-start.28 = (f32[256,16]{0,1:T(8,128)S(1)}, f32[256,16]{0,1:T(8,128)}, u32[]{:S(2)}) copy-start(f32[256,16]{0,1:T(8,128)} %param.18) | copy-start | bytes 49156
  42.2 9.9 %copy-start.14 = (bf16[128,4096]{1,0:T(8,128)(2,1)S(1)}, bf16[128,4096]{1,0:T(8,128)(2,1)}, u32[]{:S(2)}) copy-start(bf16[128,4096]{1,0:T(8,128)(2,1)} %param.13) | copy-start | bytes 3145732
  42.2 11.2 %copy-start.15 = (bf16[128,4096]{1,0:T(8,128)(2,1)S(1)}, bf16[128,4096]{1,0:T(8,128)(2,1)}, u32[]{:S(2)}) copy-start(bf16[128,4096]{1,0:T(8,128)(2,1)} %param.16) | copy-start | bytes 3145732
  45.2 313.7 %all-gather.7.cloned.1.call-start = ((), (), s32[]{:S(2)}) async-start(), calls=%async_computation.1 | async-start | bytes 4456448 | tf_op jit(solution)/shard_map/all_gather | solution.py:11
  45.4 36.5 %copy-start.7 = (f32[256,16]{1,0:T(8,128)}, f32[256,16]{1,0:T(8,128)S(1)}, u32[]{:S(2)}) copy-start(f32[256,16]{1,0:T(8,128)S(1)} %copy.86) | copy-start | bytes 49156
  52.0 29.8 %copy-start.9 = (f32[256,16]{1,0:T(8,128)}, f32[256,16]{1,0:T(8,128)S(1)}, u32[]{:S(2)}) copy-start(f32[256,16]{1,0:T(8,128)S(1)} %copy.85) | copy-start | bytes 49156
  81.9 34.4 %copy-start.2 = (bf16[4096,128]{1,0:T(8,128)(2,1)S(1)}, bf16[4096,128]{1,0:T(8,128)(2,1)}, u32[]{:S(2)}) copy-start(bf16[4096,128]{1,0:T(8,128)(2,1)} %gather_fusion) | copy-start | bytes 3145732
  81.9 34.4 %copy-start.17 = (pred[256,16]{1,0:T(8,128)(4,1)S(1)}, pred[256,16]{1,0:T(8,128)(4,1)}, u32[]{:S(2)}) copy-start(pred[256,16]{1,0:T(8,128)(4,1)} %copy-done.16) | copy-start | bytes 12292
  110.6 5.7 %copy-start = (f32[256,128,128]{2,1,0:T(8,128)}, f32[256,128,128]{2,1,0:T(8,128)S(1)}, u32[]{:S(2)}) copy-start(f32[256,128,128]{2,1,0:T(8,128)S(1)} %fusion.22) | copy-start | bytes 50331652
  139.6 15.5 %copy-start.26 = (pred[4096]{0:T(1024)(128)(4,1)S(1)}, pred[4096]{0:T(1024)(128)(4,1)}, u32[]{:S(2)}) copy-start(pred[4096]{0:T(1024)(128)(4,1)} %compare_and_fusion) | copy-start | bytes 12292
  155.1 5.1 %copy-start.21 = (s32[4096]{0:T(1024)S(1)}, s32[4096]{0:T(1024)}, u32[]{:S(2)}) copy-start(s32[4096]{0:T(1024)} %copy-done.20) | copy-start | bytes 49156
  160.2 14.2 %copy-start.25 = (pred[4096]{0:T(1024)(128)(4,1)S(1)}, pred[4096]{0:T(1024)(128)(4,1)}, u32[]{:S(2)}) copy-start(pred[4096]{0:T(1024)(128)(4,1)} %copy-done.24) | copy-start | bytes 12292
  188.5 5.6 %copy-start.3 = (f32[16,4096]{1,0:T(8,128)S(1)}, f32[16,4096]{1,0:T(8,128)}, u32[]{:S(2)}) copy-start(f32[16,4096]{1,0:T(8,128)} %get-tuple-element.137) | copy-start | bytes 786436
  195.8 6.0 %copy-start.18 = (pred[256,16]{1,0:T(8,128)(4,1)S(1)}, pred[256,16]{1,0:T(8,128)(4,1)}, u32[]{:S(2)}) copy-start(pred[256,16]{1,0:T(8,128)(4,1)} %copy-done.16) | copy-start | bytes 12292
  201.8 13.9 %copy-start.8 = (f32[256,16]{1,0:T(8,128)S(1)}, f32[256,16]{1,0:T(8,128)}, u32[]{:S(2)}) copy-start(f32[256,16]{1,0:T(8,128)} %copy-done.7) | copy-start | bytes 49156
  215.7 26.9 %copy-start.19 = (f32[16,256]{0,1:T(8,128)S(1)}, f32[16,256]{0,1:T(8,128)}, u32[]{:S(2)}) copy-start(f32[16,256]{0,1:T(8,128)} %copy.94) | copy-start | bytes 49156
  420.7 5.1 %copy-start.22 = (s32[4096]{0:T(1024)S(1)}, s32[4096]{0:T(1024)}, u32[]{:S(2)}) copy-start(s32[4096]{0:T(1024)} %fusion.52) | copy-start | bytes 49156
  425.9 14.2 %copy-start.5 = (bf16[128,4096]{0,1:T(8,128)(2,1)S(1)}, bf16[128,4096]{0,1:T(8,128)(2,1)}, u32[]{:S(2)}) copy-start(bf16[128,4096]{0,1:T(8,128)(2,1)} %copy-done.4) | copy-start | bytes 3145732
  425.9 14.2 %copy-start.27 = (pred[4096]{0:T(1024)(128)(4,1)S(1)}, pred[4096]{0:T(1024)(128)(4,1)}, u32[]{:S(2)}) copy-start(pred[4096]{0:T(1024)(128)(4,1)} %compare_and_fusion) | copy-start | bytes 12292
  (7 other events, 13.9 us)
Sparse Core Ops, SparseCore 0:
  45.3 53.8 all-gather.4
  186.4 118.6 all-gather.6
